TPU v7x, 512 devices: a whole 4x8x8 slice. The times are simulated.
512 devices in a mesh: seq: 16 (over y, x_lo), chan: 32 (over z, x_hi, core).
Axes of the slice: x: 4 (x_hi: 2, x_lo: 2; x = x_hi * 2 + x_lo), y: 8, z: 8, core: 2. Of those that a mesh axis runs over, the one named last changes fastest.
Arguments:
- stream_in: bfloat16 [2048, 8192], P('seq', 'chan'), may hold values from -64 to 64
- outer_gate: bfloat16 [2048, 8192], P('seq', 'chan'), may hold values from -4 to 4
- inner_gate: bfloat16 [2048, 8192], P('seq', 'chan'), may hold values from -4 to 4
- values: bfloat16 [2048, 8192], P('seq', 'chan'), may hold values from -4 to 4
- long_filter: bfloat16 [2048, 8192], P('seq', 'chan'), may hold values from -1.2 to 1.2
- norm_gain: float32 [8192], P('chan'), may hold values from 0.5 to 1.5
- cotangent: bfloat16 [2048, 8192], P('seq', 'chan'), may hold values from -16 to 16
Outputs:
- normed: bfloat16 [2048, 8192], P('seq', 'chan')
- stream_grad: bfloat16 [2048, 8192], P('seq', 'chan')
- outer_grad: bfloat16 [2048, 8192], P('seq', 'chan')
- inner_grad: bfloat16 [2048, 8192], P('seq', 'chan')
- value_grad: bfloat16 [2048, 8192], P('seq', 'chan')
All inputs are finite; a program needn't handle non-finite values.
Results may differ from a plain program's by a relative error of at most 0.012.
Values may be sent and summed in bfloat16 or wider, within the bound.
No kernel may reach another device: no remote copies, remote signals or barrier semaphores. Data moves between devices by JAX's collectives and lax.ppermute only.
A program may use at most 64 MiB of HBM per device.

v0:
```python
import math
import jax
import jax.numpy as jnp
from jax import lax
from jax.sharding import PartitionSpec as P

EPSILON = 1e-06
HIGHEST_MODE = lax.Precision.HIGHEST


def from_behind(value, axis, steps):
    count = lax.axis_size(axis)
    first, last = (max(0, -steps), min(count, count - steps))
    return lax.ppermute(value, axis, [(source, source + steps) for source in range(first, last)])


def shortened(shard):

    def short(part):
        return part.astype(jnp.bfloat16) if part.dtype == jnp.float32 else part

    return jax.tree.map(short, shard)


def dft_tables(half):
    length = 2 * half
    rows = lax.broadcasted_iota(jnp.int32, (length, length), 0)
    cols = lax.broadcasted_iota(jnp.int32, (length, length), 1)
    step = math.pi / half
    phase = (rows % half * cols % length).astype(jnp.float32) * step
    nyquist = (half * cols % length).astype(jnp.float32) * step
    forward = jnp.where(
        rows < half, jnp.cos(phase), jnp.where(rows == half, jnp.cos(nyquist), -jnp.sin(phase))
    )
    phase_back = (cols % half * rows % length).astype(jnp.float32) * step
    nyquist_back = (half * rows % length).astype(jnp.float32) * step
    weight = jnp.where(cols == 0, 1.0, 2.0)
    inverse = jnp.where(
        cols < half,
        weight * jnp.cos(phase_back),
        jnp.where(cols == half, jnp.cos(nyquist_back), -2.0 * jnp.sin(phase_back)),
    )
    return (forward, inverse / length)


def spectral_product(left, right, conjugate):
    half = left.shape[-2] // 2
    left_real, left_imag = (left[..., :half, :], left[..., half:, :])
    right_real, right_imag = (right[..., :half, :], right[..., half:, :])
    first_bin = lax.broadcasted_iota(jnp.int32, (half, 1), 0) == 0
    if conjugate:
        right_eff = jnp.where(first_bin, right_imag, -right_imag)
    else:
        right_eff = right_imag
    real_out = left_real * right_real - jnp.where(first_bin, 0.0, left_imag * right_eff)
    imag_out = jnp.where(
        first_bin, left_imag * right_imag, left_real * right_eff + left_imag * right_real
    )
    return jnp.concatenate([real_out, imag_out], axis=-2)


def matmul_high(left, right):
    return jnp.dot(left, right, precision=HIGHEST_MODE, preferred_element_type=jnp.float32)


def body(stream_in, outer_gate, inner_gate, values, long_filter, norm_gain, cotangent):
    half = stream_in.shape[0]
    width = stream_in.shape[1]
    forward, inverse = dft_tables(half)
    forward_half = forward[:, :half]
    outer = outer_gate.astype(jnp.float32)
    inner = inner_gate.astype(jnp.float32)
    value_rows = values.astype(jnp.float32)
    token_position = lax.axis_index("seq")
    devices = lax.axis_size("seq")
    mixed = inner * value_rows
    data_spec = matmul_high(forward_half, mixed).astype(jnp.bfloat16)
    own_spec = matmul_high(forward_half, long_filter.astype(jnp.float32)).astype(jnp.bfloat16)
    filt_spec = lax.all_gather(own_spec[None], "seq", axis=0, tiled=True)
    zero_total = jnp.zeros((2 * half, width), jnp.float32)
    piece = lax.all_gather(data_spec[None], "seq", axis=0, tiled=True)

    def forward_one_block(offset, inner_total):
        lag = token_position - offset
        taps = lax.dynamic_index_in_dim(filt_spec, jnp.clip(lag, 0, devices - 1), 0, keepdims=False)
        block = lax.dynamic_index_in_dim(piece, offset, 0, keepdims=False)
        term = spectral_product(block.astype(jnp.float32), taps.astype(jnp.float32), False)
        return inner_total + jnp.where(lag >= 0, term, 0.0)

    total = lax.fori_loop(0, piece.shape[0], forward_one_block, zero_total)
    waveform = matmul_high(inverse, total)
    spill = from_behind(waveform[half:].astype(jnp.bfloat16), "seq", 1).astype(jnp.float32)
    conv = waveform[:half] + spill
    resid = stream_in.astype(jnp.float32) + outer * conv
    scaled = cotangent.astype(jnp.float32) * norm_gain
    square_sum, proj_sum = lax.psum(
        (
            jnp.sum(resid * resid, axis=1, keepdims=True),
            jnp.sum(scaled * resid, axis=1, keepdims=True),
        ),
        "chan",
    )
    total_width = width * lax.axis_size("chan")
    inv_rms = lax.rsqrt(square_sum / total_width + EPSILON)
    normed = (resid * inv_rms * norm_gain).astype(jnp.bfloat16)
    grad_resid = inv_rms * (scaled - resid * inv_rms * inv_rms * (proj_sum / total_width))
    outer_grad = (grad_resid * conv).astype(jnp.bfloat16)
    dconv = grad_resid * outer
    following = from_behind(shortened(dconv), "seq", -1).astype(dconv.dtype)
    back_spec = matmul_high(forward, jnp.concatenate([dconv, following], axis=0)).astype(
        jnp.bfloat16
    )
    backward_piece = lax.all_gather(back_spec[None], "seq", axis=0, tiled=True)

    def backward_one_block(offset, inner_total):
        lag = offset - token_position
        taps = lax.dynamic_index_in_dim(filt_spec, jnp.clip(lag, 0, devices - 1), 0, keepdims=False)
        block = lax.dynamic_index_in_dim(backward_piece, offset, 0, keepdims=False)
        term = spectral_product(block.astype(jnp.float32), taps.astype(jnp.float32), True)
        return inner_total + jnp.where(lag >= 0, term, 0.0)

    back_total = lax.fori_loop(
        0, backward_piece.shape[0], backward_one_block, jnp.zeros((2 * half, width), jnp.float32)
    )
    dmixed = matmul_high(inverse[:half], back_total)
    inner_grad = (dmixed * value_rows).astype(jnp.bfloat16)
    value_grad = (dmixed * inner).astype(jnp.bfloat16)
    return (normed, grad_resid.astype(jnp.bfloat16), outer_grad, inner_grad, value_grad)


def solution(mesh):
    placed = (
        P("seq", "chan"),
        P("seq", "chan"),
        P("seq", "chan"),
        P("seq", "chan"),
        P("seq", "chan"),
        P("chan"),
        P("seq", "chan"),
    )
    return jax.shard_map(
        body,
        mesh=mesh,
        in_specs=placed,
        out_specs=(
            P("seq", "chan"),
            P("seq", "chan"),
            P("seq", "chan"),
            P("seq", "chan"),
            P("seq", "chan"),
        ),
        check_vma=False,
    )
```

profile of v0, /device:TPU:4, one launch (start us, length us, event | category | flops | bytes accessed | tf_op | source)
XLA Modules:
  0.0 370.6 jit_solution(12434627319497629787)
XLA Ops:
  7.3 2.7 select_multiply_fusion
  11.0 1.9 convolution_convert_fusion.2
  13.0 77.7 %all-gather.9.cloned.1.call-done = bf16[4096,256]{1,0:T(8,128)(2,1)} async-done(((bf16[256,256]{1,0:T(8,128)(2,1)}), bf16[4096,256]{1,0:T(8,128)(2,1)}) %all-gather.9.cloned.1.call-update) | async-done | bytes 2097168 | tf_op jit(solution)/shard_map/all_gather | solution.py:79
  90.7 76.4 %all-gather.7.cloned.1.call-done = bf16[4096,256]{1,0:T(8,128)(2,1)} async-done(((bf16[256,256]{1,0:T(8,128)(2,1)}), bf16[4096,256]{1,0:T(8,128)(2,1)}) %all-gather.7.cloned.1.call-update) | async-done | bytes 2097168 | tf_op jit(solution)/shard_map/all_gather | solution.py:81
  167.0 19.8 %while.28 = (s32[]{:T(128)}, f32[256,256]{1,0:T(8,128)S(1)}, s32[]{:T(128)}, bf16[16,256,256]{2,1,0:T(8,128)(2,1)}, bf16[16,256,256]{2,1,0:T(8,128)(2,1)}, /*index=5*/s32[]{:T(128)}, s32[]{:T(128)}, s32[]{:T(128)}) while((s32[]{:T(128)}, f32[256,256]{1,0:T(8,128)S(1)}, s32[]{:T(128)}, bf16[16,256,256]{2,1,0:T(8,128)(2,1)}, ...), condition=%wide.region_1.2_spmd.clone, body=%wide.region_0.1_spmd.clone.sunk | while | flops 655495 | bytes 2359701 | solution.py:90
  168.3 1.0 dynamic-slice_convert_fusion.6
  169.5 1.0 dynamic-slice_convert_fusion.6
  170.7 1.0 dynamic-slice_convert_fusion.6
  179.4 1.0 dynamic-slice_convert_fusion.6
  180.7 1.0 dynamic-slice_convert_fusion.6
  181.9 1.0 dynamic-slice_convert_fusion.6
  183.1 1.0 dynamic-slice_convert_fusion.6
  184.4 1.0 dynamic-slice_convert_fusion.6
  185.6 1.0 dynamic-slice_convert_fusion.6
  186.9 2.2 fusion.23
  189.1 1.5 collective-permute-start
  191.0 1.5 collective-permute-done
  192.6 60.3 %all-reduce = (f32[128,1]{0,1:T(1,128)S(1)}, f32[128,1]{0,1:T(1,128)S(1)}) all-reduce(f32[128,1]{0,1:T(1,128)S(1)} %bitcast.65, f32[128,1]{0,1:T(1,128)S(1)} %bitcast.64), channel_id=1, replica_groups=mesh['seq'=16,'chan'=32] {'chan'}, use_global_device_ids=true, to_apply=%region_3.4 | all-reduce | flops 256 | bytes 2048 | tf_op jit(solution)/shard_map/psum | solution.py:96
  253.1 1.3 collective-permute-start.1
  254.4 5.6 %collective-permute-done.1 = bf16[128,256]{0,1:T(8,128)(2,1)S(1)} collective-permute-done((bf16[128,256]{0,1:T(8,128)(2,1)S(1)}, bf16[128,256]{0,1:T(8,128)(2,1)S(1)}, u32[]{:S(2)}, u32[]{:S(2)}) %collective-permute-start.1) | collective-permute-done | bytes 65568 | tf_op jit(solution)/shard_map/ppermute | solution.py:14
  260.0 2.2 convolution_convert_fusion
  264.5 78.4 %all-gather.11.cloned.1.call-done = bf16[4096,256]{1,0:T(8,128)(2,1)} async-done(((bf16[256,256]{1,0:T(8,128)(2,1)}), bf16[4096,256]{1,0:T(8,128)(2,1)}) %all-gather.11.cloned.1.call-update) | async-done | bytes 2097168 | tf_op jit(solution)/shard_map/all_gather | solution.py:113
  343.0 20.1 %while.29 = (s32[]{:T(128)}, f32[256,256]{1,0:T(8,128)S(1)}, s32[]{:T(128)}, bf16[16,256,256]{2,1,0:T(8,128)(2,1)}, bf16[16,256,256]{2,1,0:T(8,128)(2,1)}, /*index=5*/s32[]{:T(128)}, s32[]{:T(128)}, s32[]{:T(128)}) while((s32[]{:T(128)}, f32[256,256]{1,0:T(8,128)S(1)}, s32[]{:T(128)}, bf16[16,256,256]{2,1,0:T(8,128)(2,1)}, ...), condition=%wide.region_7.8_spmd.clone, body=%wide.region_6.7_spmd.clone.sunk | while | flops 753799 | bytes 2359701 | solution.py:122
  343.0 1.0 dynamic-slice_convert_fusion.7
  (159 shorter events, 33.0 us)
Async XLA Ops:
  7.2 2.8 copy-start
  7.2 83.5 %all-gather.9.cloned.1.call-start = ((), (), s32[]{:S(2)}) async-start(), calls=%async_computation.1 | async-start | bytes 2228224 | tf_op jit(solution)/shard_map/all_gather | solution.py:79
  10.9 156.1 %all-gather.7.cloned.1.call-start = ((), (), s32[]{:S(2)}) async-start(), calls=%async_computation | async-start | bytes 2228224 | tf_op jit(solution)/shard_map/all_gather | solution.py:81
  12.9 330.1 %all-gather.11.cloned.1.call-start = ((), (), s32[]{:S(2)}) async-start(), calls=%async_computation.2 | async-start | bytes 2228224 | tf_op jit(solution)/shard_map/all_gather | solution.py:113
  186.8 3.8 %copy-start.3 = (bf16[128,256]{1,0:T(8,128)(2,1)S(1)}, bf16[128,256]{1,0:T(8,128)(2,1)}, u32[]{:S(2)}) copy-start(bf16[128,256]{1,0:T(8,128)(2,1)} %param.12) | copy-start | bytes 196612
  186.8 3.9 %copy-start.4 = (bf16[128,256]{1,0:T(8,128)(2,1)S(1)}, bf16[128,256]{1,0:T(8,128)(2,1)}, u32[]{:S(2)}) copy-start(bf16[128,256]{1,0:T(8,128)(2,1)} %param.17) | copy-start | bytes 196612
  186.9 4.0 %copy-start.5 = (bf16[128,256]{1,0:T(8,128)(2,1)S(1)}, bf16[128,256]{1,0:T(8,128)(2,1)}, u32[]{:S(2)}) copy-start(bf16[128,256]{1,0:T(8,128)(2,1)} %param.11) | copy-start | bytes 196612
  186.9 5.6 %copy-start.6 = (f32[256]{0:T(256)S(1)}, f32[256]{0:T(256)}, u32[]{:S(2)}) copy-start(f32[256]{0:T(256)} %param.16) | copy-start | bytes 3076
  189.1 3.4 collective-permute-start
  253.1 6.9 %collective-permute-start.1 = (bf16[128,256]{0,1:T(8,128)(2,1)S(1)}, bf16[128,256]{0,1:T(8,128)(2,1)S(1)}, u32[]{:S(2)}, u32[]{:S(2)}) collective-permute-start(bf16[128,256]{0,1:T(8,128)(2,1)S(1)} %get-tuple-element.260), channel_id=1, source_target_pairs={{32,0},{64,32},{96,64},{128,96},{160,128},{192,160},{224,192},{256... | collective-permute-start | bytes 196616 | tf_op jit(solution)/shard_map/ppermute | solution.py:14
  343.0 20.1 %copy-start.1 = (bf16[128,256]{1,0:T(8,128)(2,1)S(1)}, bf16[128,256]{1,0:T(8,128)(2,1)}, u32[]{:S(2)}) copy-start(bf16[128,256]{1,0:T(8,128)(2,1)} %param.14) | copy-start | bytes 196612
  343.0 20.1 %copy-start.2 = (bf16[128,256]{1,0:T(8,128)(2,1)S(1)}, bf16[128,256]{1,0:T(8,128)(2,1)}, u32[]{:S(2)}) copy-start(bf16[128,256]{1,0:T(8,128)(2,1)} %param.13) | copy-start | bytes 196612
Sparse Core Ops, SparseCore 0:
  11.0 79.5 all-gather.8
  92.8 74.2 all-gather.6
  262.4 80.5 all-gather.10
where the time goes:
time: 371 us
  waiting for transfers between devices  240 us (65%)
  blocking collectives  60.3 us (16%)
  other arithmetic  41.2 us (11%)
  between operations  14 us (4%)
  matrix products  8.16 us (2%)
    all_gather x1, waiting for transfers between devices, body(): backward_piece = lax.all_gather(back_spec[None], 'seq', axis=0, tiled=True)  78.4 us
    all_gather x1, waiting for transfers between devices, body(): filt_spec = lax.all_gather(own_spec[None], 'seq', axis=0, tiled=True)  77.7 us
    all_gather x1, waiting for transfers between devices, body(): piece = lax.all_gather(data_spec[None], 'seq', axis=0, tiled=True)  76.4 us
    psum x1, blocking collectives, body(): lax.psum((jnp.sum(resid * resid, axis=1, keepdims=True), jnp.sum(scaled *...  60.3 us
    convert_element_type x16, other arithmetic, backward_one_block(): taps.astype(jnp.float32)  16.2 us
    convert_element_type x16, other arithmetic, forward_one_block(): taps.astype(jnp.float32)  16.2 us
    dot_general x5, matrix products, matmul_high(): jnp.dot(left, right, precision=HIGHEST_MODE, preferred_element_type=jnp.f...  8.16 us
  transfers between devices with their start and end apart: 5, of which 5 were waited for; matrix products, arithmetic and copies ran while one was open for 1% of the time, Pallas kernels for 0%

commit v1 on v0

--- a/solution.py
+++ b/solution.py
@@ -76,7 +76,10 @@
     mixed = inner * value_rows
     data_spec = matmul_high(forward_half, mixed).astype(jnp.bfloat16)
     own_spec = matmul_high(forward_half, long_filter.astype(jnp.float32)).astype(jnp.bfloat16)
-    filt_spec = lax.all_gather(own_spec[None], "seq", axis=0, tiled=True)
+    buf = own_spec[None]
+    e_now = jnp.stack([buf for _ in range(lax.axis_size("seq"))], axis=0)
+    near = lax.all_to_all(e_now, "seq", 0, 0)
+    filt_spec = jnp.concatenate(near, 0)
     zero_total = jnp.zeros((2 * half, width), jnp.float32)
     piece = lax.all_gather(data_spec[None], "seq", axis=0, tiled=True)
 

time: 371 us -> 325 us (0.88)
  waiting for transfers between devices: 240 us -> 185 us
  starting transfers between devices: 2.94 us -> 10.9 us
    all_gather x1 -> x0, waiting for transfers between devices: 77.7 us -> none  [body(): filt_spec = lax.all_gather(own_spec[None], 'seq', axis=0, tiled=True)]
    all_to_all x0 -> x1, waiting for transfers between devices: none -> 52.5 us  [body(): near = lax.all_to_all(e_now, 'seq', 0, 0)]
    all_gather x1, waiting for transfers between devices: 76.4 us -> 48.9 us  [body(): piece = lax.all_gather(data_spec[None], 'seq', axis=0, tiled=True)]
    all_to_all x0 -> x1, starting transfers between devices: none -> 7.97 us  [body(): near = lax.all_to_all(e_now, 'seq', 0, 0)]
where the time goes in v1:
time: 325 us; the launch traced here: 324 us
  waiting for transfers between devices  185 us (57%)
  blocking collectives  62.1 us (19%)
  other arithmetic  39.1 us (12%)
  between operations  14.3 us (4%)
  starting transfers between devices  10.9 us (3%)
  matrix products  6.61 us (2%)
  local copies, waits for them, and re-layouts  4.11 us (1%)
    all_gather x1, waiting for transfers between devices, body(): backward_piece = lax.all_gather(back_spec[None], 'seq', axis=0, tiled=True)  76.5 us
    psum x1, blocking collectives, body(): lax.psum((jnp.sum(resid * resid, axis=1, keepdims=True), jnp.sum(scaled *...  62.1 us
    all_to_all x1, waiting for transfers between devices, body(): near = lax.all_to_all(e_now, 'seq', 0, 0)  52.5 us
    all_gather x1, waiting for transfers between devices, body(): piece = lax.all_gather(data_spec[None], 'seq', axis=0, tiled=True)  48.9 us
    convert_element_type x16, other arithmetic, backward_one_block(): taps.astype(jnp.float32)  15.1 us
    convert_element_type x16, other arithmetic, forward_one_block(): taps.astype(jnp.float32)  15.1 us
    all_to_all x1, starting transfers between devices, body(): near = lax.all_to_all(e_now, 'seq', 0, 0)  7.97 us
    ppermute x2, waiting for transfers between devices, from_behind(): lax.ppermute(value, axis, [(source, source + steps) for source in range(f...  7.06 us
  transfers between devices with their start and end apart: 5, of which 5 were waited for; matrix products, arithmetic and copies ran while one was open for 1% of the time, Pallas kernels for 0%

profile of v1, /device:TPU:4, one launch (start us, length us, event | category | flops | bytes accessed | tf_op | source)
XLA Modules:
  0.0 323.8 jit_solution(7542669787765009900)
XLA Ops:
  7.2 2.7 select_multiply_fusion
  10.2 1.5 stack.3
  11.7 8.0 %all-to-all-start = ((bf16[16,1,256,256]{3,2,1,0:T(8,128)(2,1)}), bf16[16,1,256,256]{3,2,1,0:T(8,128)(2,1)S(1)}, u32[]{:S(2)}, u32[]{:S(2)}) async-start(bf16[16,1,256,256]{3,2,1,0:T(8,128)(2,1)} %stack.3), calls=%async_computation | async-start | bytes 4194304 | tf_op jit(solution)/shard_map/all_to_all | solution.py:81
  19.8 1.0 convolution_convert_fusion.2
  20.9 52.5 %all-to-all-done = bf16[16,1,256,256]{3,2,1,0:T(8,128)(2,1)S(1)} async-done(((bf16[16,1,256,256]{3,2,1,0:T(8,128)(2,1)}), bf16[16,1,256,256]{3,2,1,0:T(8,128)(2,1)S(1)}, u32[]{:S(2)}, u32[]{:S(2)}) %all-to-all-start) | async-done | bytes 2097184 | tf_op jit(solution)/shard_map/all_to_all | solution.py:81
  73.4 48.9 %all-gather.5.cloned.1.call-done = bf16[4096,256]{1,0:T(8,128)(2,1)} async-done(((bf16[256,256]{1,0:T(8,128)(2,1)}), bf16[4096,256]{1,0:T(8,128)(2,1)}) %all-gather.5.cloned.1.call-update) | async-done | bytes 2097168 | tf_op jit(solution)/shard_map/all_gather | solution.py:84
  122.3 18.8 %while.28 = (s32[]{:T(128)}, f32[256,256]{1,0:T(8,128)S(1)}, s32[]{:T(128)}, bf16[16,256,256]{2,1,0:T(8,128)(2,1)}, bf16[16,256,256]{2,1,0:T(8,128)(2,1)S(1)}, /*index=5*/s32[]{:T(128)}, s32[]{:T(128)}, s32[]{:T(128)}) while((s32[]{:T(128)}, f32[256,256]{1,0:T(8,128)S(1)}, s32[]{:T(128)}, bf16[16,256,256]{2,1,0:T(8,128)(2,1)}, ...), condition=%wide.region_1.2_spmd.clone, body=%wide.region_0.1_spmd.clone.sunk | while | flops 655495 | bytes 2359701 | solution.py:93
  123.5 0.9 dynamic-slice_convert_fusion.6
  125.8 0.9 dynamic-slice_convert_fusion.6
  128.2 0.9 dynamic-slice_convert_fusion.6
  130.5 0.9 dynamic-slice_convert_fusion.6
  132.9 0.9 dynamic-slice_convert_fusion.6
  134.0 0.9 dynamic-slice_convert_fusion.6
  135.2 0.9 dynamic-slice_convert_fusion.6
  136.4 0.9 dynamic-slice_convert_fusion.6
  141.1 2.2 fusion.23
  143.3 1.6 collective-permute-start
  145.2 1.5 collective-permute-done
  146.9 62.1 %all-reduce = (f32[128,1]{0,1:T(1,128)S(1)}, f32[128,1]{0,1:T(1,128)S(1)}) all-reduce(f32[128,1]{0,1:T(1,128)S(1)} %bitcast.65, f32[128,1]{0,1:T(1,128)S(1)} %bitcast.64), channel_id=1, replica_groups=mesh['seq'=16,'chan'=32] {'chan'}, use_global_device_ids=true, to_apply=%region_3.4 | all-reduce | flops 256 | bytes 2048 | tf_op jit(solution)/shard_map/psum | solution.py:99
  209.1 1.3 collective-permute-start.1
  210.4 5.6 %collective-permute-done.1 = bf16[128,256]{0,1:T(8,128)(2,1)S(1)} collective-permute-done((bf16[128,256]{0,1:T(8,128)(2,1)S(1)}, bf16[128,256]{0,1:T(8,128)(2,1)S(1)}, u32[]{:S(2)}, u32[]{:S(2)}) %collective-permute-start.1) | collective-permute-done | bytes 65568 | tf_op jit(solution)/shard_map/ppermute | solution.py:14
  216.0 2.2 convolution_convert_fusion
  220.5 76.5 %all-gather.7.cloned.1.call-done = bf16[4096,256]{1,0:T(8,128)(2,1)} async-done(((bf16[256,256]{1,0:T(8,128)(2,1)}), bf16[4096,256]{1,0:T(8,128)(2,1)}) %all-gather.7.cloned.1.call-update) | async-done | bytes 2097168 | tf_op jit(solution)/shard_map/all_gather | solution.py:116
  297.0 19.1 %while.29 = (s32[]{:T(128)}, f32[256,256]{1,0:T(8,128)S(1)}, s32[]{:T(128)}, bf16[16,256,256]{2,1,0:T(8,128)(2,1)}, bf16[16,256,256]{2,1,0:T(8,128)(2,1)S(1)}, /*index=5*/s32[]{:T(128)}, s32[]{:T(128)}, s32[]{:T(128)}) while((s32[]{:T(128)}, f32[256,256]{1,0:T(8,128)S(1)}, s32[]{:T(128)}, bf16[16,256,256]{2,1,0:T(8,128)(2,1)}, ...), condition=%wide.region_7.8_spmd.clone, body=%wide.region_6.7_spmd.clone.sunk | while | flops 753799 | bytes 2359701 | solution.py:125
  (159 shorter events, 32.8 us)
Async XLA Ops:
  7.2 2.8 copy-start
  11.7 8.0 %copy-start.1 = (bf16[128,256]{1,0:T(8,128)(2,1)S(1)}, bf16[128,256]{1,0:T(8,128)(2,1)}, u32[]{:S(2)}) copy-start(bf16[128,256]{1,0:T(8,128)(2,1)} %param.14) | copy-start | bytes 196612
  11.7 8.0 %copy-start.2 = (bf16[128,256]{1,0:T(8,128)(2,1)S(1)}, bf16[128,256]{1,0:T(8,128)(2,1)}, u32[]{:S(2)}) copy-start(bf16[128,256]{1,0:T(8,128)(2,1)} %param.13) | copy-start | bytes 196612
  11.7 61.7 %all-to-all-start = ((bf16[16,1,256,256]{3,2,1,0:T(8,128)(2,1)}), bf16[16,1,256,256]{3,2,1,0:T(8,128)(2,1)S(1)}, u32[]{:S(2)}, u32[]{:S(2)}) async-start(bf16[16,1,256,256]{3,2,1,0:T(8,128)(2,1)} %stack.3), calls=%async_computation | async-start | bytes 4194304 | tf_op jit(solution)/shard_map/all_to_all | solution.py:81
  19.7 102.6 %all-gather.5.cloned.1.call-start = ((), (), s32[]{:S(2)}) async-start(), calls=%async_computation.1 | async-start | bytes 2228224 | tf_op jit(solution)/shard_map/all_gather | solution.py:84
  20.8 276.2 %all-gather.7.cloned.1.call-start = ((), (), s32[]{:S(2)}) async-start(), calls=%async_computation.2 | async-start | bytes 2228224 | tf_op jit(solution)/shard_map/all_gather | solution.py:116
  141.1 3.8 %copy-start.3 = (bf16[128,256]{1,0:T(8,128)(2,1)S(1)}, bf16[128,256]{1,0:T(8,128)(2,1)}, u32[]{:S(2)}) copy-start(bf16[128,256]{1,0:T(8,128)(2,1)} %param.12) | copy-start | bytes 196612
  141.1 3.9 %copy-start.4 = (bf16[128,256]{1,0:T(8,128)(2,1)S(1)}, bf16[128,256]{1,0:T(8,128)(2,1)}, u32[]{:S(2)}) copy-start(bf16[128,256]{1,0:T(8,128)(2,1)} %param.17) | copy-start | bytes 196612
  141.1 4.0 %copy-start.5 = (bf16[128,256]{1,0:T(8,128)(2,1)S(1)}, bf16[128,256]{1,0:T(8,128)(2,1)}, u32[]{:S(2)}) copy-start(bf16[128,256]{1,0:T(8,128)(2,1)} %param.11) | copy-start | bytes 196612
  141.1 5.6 %copy-start.6 = (f32[256]{0:T(256)S(1)}, f32[256]{0:T(256)}, u32[]{:S(2)}) copy-start(f32[256]{0:T(256)} %param.16) | copy-start | bytes 3076
  143.3 3.4 %collective-permute-start = (bf16[128,256]{0,1:T(8,128)(2,1)S(1)}, bf16[128,256]{0,1:T(8,128)(2,1)S(1)}, u32[]{:S(2)}, u32[]{:S(2)}) collective-permute-start(bf16[128,256]{0,1:T(8,128)(2,1)S(1)} %slice.167), channel_id=1, source_target_pairs={{0,32},{32,64},{64,96},{96,128},{128,160},{160,192},{192,224},{224... | collective-permute-start | bytes 196616 | tf_op jit(solution)/shard_map/ppermute | solution.py:14
  209.1 6.9 %collective-permute-start.1 = (bf16[128,256]{0,1:T(8,128)(2,1)S(1)}, bf16[128,256]{0,1:T(8,128)(2,1)S(1)}, u32[]{:S(2)}, u32[]{:S(2)}) collective-permute-start(bf16[128,256]{0,1:T(8,128)(2,1)S(1)} %get-tuple-element.265), channel_id=1, source_target_pairs={{32,0},{64,32},{96,64},{128,96},{160,128},{192,160},{224,192},{256... | collective-permute-start | bytes 196616 | tf_op jit(solution)/shard_map/ppermute | solution.py:14
Sparse Core Ops, SparseCore 0:
  22.6 99.6 all-gather.4
  218.4 78.5 all-gather.6
